TPU v7x, 512 devices: a whole 4x4x16 slice. The times are simulated.
512 devices in a mesh: section: 32 (over z_hi, y, core), tp: 16 (over z_lo, x).
Axes of the slice: x: 4, y: 4, z: 16 (z_hi: 4, z_lo: 4; z = z_hi * 4 + z_lo), core: 2. Of those that a mesh axis runs over, the one named last changes fastest.
Arguments:
- grad_in: bfloat16 [32, 160, 8192], P('section', None, 'tp'), may hold values from -6 to 6
- out_proj: bfloat16 [32, 4096, 8192], P('section', 'tp'), may hold values from -0.09375 to 0.09375
- value_proj: bfloat16 [32, 8192, 512], P('section', 'tp'), may hold values from -0.0625 to 0.0625
- head_delta: bfloat16 [32, 160, 4096], P('section', None, 'tp'), may hold values from -6 to 6
- pattern: bfloat16 [32, 32, 160, 160], P('section', 'tp'), may hold values from 0 to 0.25
- positions: int32 [160], replicated, may hold values from -1 to 31, as said below
- node_map: int32 [32, 32], P('section'), may hold values from 0 to 31, each once within a row
Outputs:
- residual_grad: bfloat16 [32, 160, 8192], P('section', None, 'tp')
- edge_scores: float32 [32, 32, 32], P('section')
Inputs may be any that keep to these rules, and one draw needn't show every extreme that they name: positions[t] = (t mod 32) - p, or -1 where that is negative, with one left padding p of 0 to 15 for each block of 32 tokens; the first block is unpadded. `node_map`: each row names every node once.
All inputs are finite; a program needn't handle non-finite values.
Results may differ from a plain program's by a relative error of at most 0.0095.
Values may be sent and summed in bfloat16 or wider, within the bound.
No kernel may reach another device: no remote copies, remote signals or barrier semaphores. Data moves between devices by JAX's collectives and lax.ppermute only.
A program may use at most 128 MiB of HBM per device.

v0:
```python
import jax
import jax.numpy as jnp
from jax import lax
from jax.sharding import PartitionSpec as P

HEADS = 32
HEAD_DIM = 128
KV = 4
PROMPT = 32
GROUP = 8


def on_device(grad_in, out_proj, value_proj, head_delta, pattern, positions, node_map):
    tokens = grad_in.shape[1]
    local_width = grad_in.shape[2]
    own_rows = out_proj.shape[1]
    own_heads = own_rows // HEAD_DIM
    width = out_proj.shape[2]
    tp_count = lax.axis_size("tp")
    section_count = lax.axis_size("section")
    weights = out_proj[0]
    blocks = weights.reshape(own_rows, tp_count, width // tp_count).transpose(1, 0, 2)
    column_blocks = lax.all_to_all(blocks, "tp", 0, 0, tiled=True)
    all_delta_cols = lax.all_gather(head_delta[0], "tp", axis=1, tiled=True)
    token_ids = jnp.arange(tokens)
    block_ids = token_ids // PROMPT
    allowed = (
        (block_ids[:, None] == block_ids[None, :])
        & (positions[None, :] >= 0)
        & (positions[None, :] <= positions[:, None])
    )
    visible = allowed.astype(jnp.bfloat16)
    grad_rows = lax.all_gather(grad_in[0], "tp", axis=1, tiled=True)
    head_grad = lax.dot_general(
        grad_rows, weights, (((1,), (1,)), ((), ())), preferred_element_type=jnp.float32
    ).astype(jnp.bfloat16)
    masked = pattern[0] * visible[None]
    value_grad = jnp.einsum(
        "hts,thc->shc",
        masked,
        head_grad.reshape(tokens, own_heads, HEAD_DIM),
        preferred_element_type=jnp.float32,
    ).astype(jnp.bfloat16)
    pair_sum = value_grad.astype(jnp.float32).sum(axis=1)
    group_of = lax.axis_index("tp") * own_heads // GROUP
    slots = jnp.zeros((tokens, KV, HEAD_DIM), jnp.float32)
    slots = lax.dynamic_update_slice(slots, pair_sum[:, None, :], (0, group_of, 0))
    summed = lax.psum(slots, "tp")
    group_grad = summed.reshape(tokens, KV * HEAD_DIM).astype(jnp.bfloat16)
    increment = lax.dot_general(
        group_grad, value_proj[0], (((1,), (1,)), ((), ())), preferred_element_type=jnp.float32
    )
    residual_grad = (grad_in[0].astype(jnp.float32) + increment).astype(jnp.bfloat16)
    target_row = increment.astype(jnp.bfloat16)
    target_rows = lax.all_gather(target_row[None], "section", axis=0, tiled=True)
    delta = jnp.einsum(
        "thc,hcd->htd",
        all_delta_cols.reshape(tokens, HEADS, HEAD_DIM),
        column_blocks.reshape(HEADS, HEAD_DIM, local_width),
        preferred_element_type=jnp.float32,
    ).astype(jnp.bfloat16)
    partial_scores = lax.dot_general(
        delta.reshape(HEADS, tokens * local_width),
        target_rows.reshape(section_count, tokens * local_width),
        (((1,), (1,)), ((), ())),
        preferred_element_type=jnp.float32,
    )
    totals = lax.psum(partial_scores, "tp")
    later = jnp.arange(section_count) > lax.axis_index("section")
    raw_scores = jnp.where(later[None, :], totals / tokens, jnp.zeros_like(totals))
    onehot = (node_map[0][:, None] == jnp.arange(HEADS)[None, :]).astype(jnp.float32)
    edge_scores = jnp.dot(onehot.T, raw_scores, precision=lax.Precision.HIGHEST)
    return (residual_grad[None], edge_scores[None])


def solution(mesh):
    placed = (
        P("section", None, "tp"),
        P("section", "tp", None),
        P("section", "tp", None),
        P("section", None, "tp"),
        P("section", "tp", None, None),
        P(),
        P("section", None),
    )
    return jax.shard_map(
        on_device,
        mesh=mesh,
        in_specs=placed,
        out_specs=(P("section", None, "tp"), P("section", None, None)),
        check_vma=False,
    )
```

profile of v0, /device:TPU:8, one launch (start us, length us, event | category | flops | bytes accessed | tf_op | source)
XLA Modules:
  0.0 441.4 jit_solution(2010720892174601740)
XLA Ops:
  7.2 0.0 copy-start
  7.2 0.0 all-gather.7.cloned.1.call-start
  7.2 0.7 all-gather.7.cloned.1.call-update
  7.9 6.4 %copy.21 = bf16[1,256,8192]{1,2,0:T(8,128)(2,1)} copy(bf16[1,256,8192]{2,1,0:T(8,128)(2,1)} %param.8) | data formatting | bytes 8388608 | tf_op args[1]
  14.3 8.6 %all-to-all-start = ((bf16[16,256,512]{1,2,0:T(8,128)(2,1)}), bf16[16,256,512]{1,2,0:T(8,128)(2,1)}, u32[]{:S(2)}, u32[]{:S(2)}) async-start(bf16[16,256,512]{1,2,0:T(8,128)(2,1)} %bitcast.55), calls=%async_computation | async-start | bytes 8388608 | tf_op jit(solution)/shard_map/all_to_all | solution.py:23
  23.0 0.0 all-gather.9.cloned.1.call-start
  23.0 0.7 all-gather.9.cloned.1.call-update
  23.7 0.0 all-gather.11.cloned.1.call-start
  23.8 0.0 copy-done.3
  23.8 0.1 and_convert_fusion
  24.0 0.0 copy-start.2
  24.0 0.0 copy-start.1
  24.0 125.0 %all-gather.7.cloned.1.call-done = bf16[1,160,8192]{2,1,0:T(8,128)(2,1)} async-done(((bf16[1,160,512]{2,1,0:T(8,128)(2,1)}), bf16[1,160,8192]{2,1,0:T(8,128)(2,1)}) %all-gather.7.cloned.1.call-update) | async-done | bytes 2621456 | tf_op jit(solution)/shard_map/all_gather | solution.py:33
  149.0 4.5 %fusion.14 = bf16[20,2,8,128]{3,2,1,0:T(8,128)(2,1)S(1)} fusion(bf16[1,256,8192]{2,1,0:T(8,128)(2,1)} %param.8, bf16[1,160,8192]{2,1,0:T(8,128)(2,1)} %all-gather.7.cloned.1.call-done), kind=kOutput, calls=%fused_computation.12 | convolution fusion | flops 671129600 | bytes 6897664 | tf_op jit(solution)/shard_map/dot_general | solution.py:34
  153.5 0.0 copy-done.2
  153.5 0.2 fusion.13
  153.8 2.7 dynamic_update_slice.3
  156.6 78.9 %all-reduce.1 = bf16[160,4,128]{2,1,0:T(4,128)(2,1)S(1)} all-reduce(f32[160,4,128]{2,1,0:T(4,128)S(1)} %dynamic_update_slice.3), channel_id=1, replica_groups=mesh['section'=32,'tp'=16] {'tp'}, use_global_device_ids=true, to_apply=%region_1.2 | all-reduce | flops 81920 | bytes 491520 | tf_op jit(solution)/shard_map/psum | solution.py:48
  235.5 0.0 copy-done
  235.5 0.0 copy-done.1
  235.5 1.0 fusion.41
  236.6 0.0 all-gather.11.cloned.1.call-update
  236.6 0.0 all-gather.9.cloned.1.call-done
  236.6 1.6 copy.29
  238.2 0.0 all-to-all-done
  238.2 6.4 %copy.22 = bf16[16,256,512]{2,1,0:T(8,128)(2,1)} copy(bf16[16,256,512]{1,2,0:T(8,128)(2,1)} %all-to-all-done) | data formatting | bytes 8388608 | tf_op jit(solution)/shard_map/all_to_all | solution.py:23
  244.6 6.0 %convolution_convert_fusion = bf16[32,160,512]{2,1,0:T(8,128)(2,1)} fusion(bf16[32,128,512]{2,1,0:T(8,128)(2,1)} %bitcast.56, bf16[160,32,128]{2,1,0:T(8,128)(2,1)S(1)} %bitcast.57), kind=kOutput, calls=%fused_computation.5 | convolution fusion | flops 673710080 | bytes 10747904 | tf_op jit(solution)/shard_map/thc,hcd->htd/dot_general | solution.py:56
  250.7 92.8 %all-gather.11.cloned.1.call-done = bf16[5120,512]{1,0:T(8,128)(2,1)} async-done(((bf16[160,512]{1,0:T(8,128)(2,1)}), bf16[5120,512]{1,0:T(8,128)(2,1)}) %all-gather.11.cloned.1.call-update) | async-done | bytes 5242896 | tf_op jit(solution)/shard_map/all_gather | solution.py:55
  343.5 15.0 %fusion.19 = f32[32,32]{1,0:T(8,128)S(1)} fusion(bf16[32,160,512]{2,1,0:T(8,128)(2,1)} %bitcast.61, bf16[32,160,512]{2,1,0:T(8,128)(2,1)} %convolution_convert_fusion), kind=kOutput, calls=%fused_computation.13 | convolution fusion | flops 167772160 | bytes 10489856 | tf_op jit(solution)/shard_map/dot_general | solution.py:62
  358.5 75.6 %psum.15 = f32[32,32]{1,0:T(8,128)S(1)} all-reduce(f32[32,32]{1,0:T(8,128)S(1)} %fusion.19), channel_id=1, replica_groups=mesh['section'=32,'tp'=16] {'tp'}, use_global_device_ids=true, to_apply=%region_2.3 | all-reduce | flops 1024 | bytes 8192 | tf_op jit(solution)/shard_map/psum | solution.py:68
  434.0 0.0 copy-done.4
  434.0 0.9 convolution_bitcast_fusion
  (6 shorter events, 0.1 us)
Async XLA Ops:
  7.2 228.3 %copy-start = (bf16[1,512,512]{2,1,0:T(8,128)(2,1)S(1)}, bf16[1,512,512]{2,1,0:T(8,128)(2,1)}, u32[]{:S(2)}) copy-start(bf16[1,512,512]{2,1,0:T(8,128)(2,1)} %param.9) | copy-start | bytes 1572868
  7.2 141.8 %all-gather.7.cloned.1.call-start = ((), (), s32[]{:S(2)}) async-start(), calls=%async_computation.1 | async-start | bytes 2785280 | tf_op jit(solution)/shard_map/all_gather | solution.py:33
  14.3 9.5 %copy-start.3 = (s32[160]{0:T(256)S(1)}, s32[160]{0:T(256)}, u32[]{:S(2)}) copy-start(s32[160]{0:T(256)} %param.12) | copy-start | bytes 1924
  14.3 223.9 %all-to-all-start = ((bf16[16,256,512]{1,2,0:T(8,128)(2,1)}), bf16[16,256,512]{1,2,0:T(8,128)(2,1)}, u32[]{:S(2)}, u32[]{:S(2)}) async-start(bf16[16,256,512]{1,2,0:T(8,128)(2,1)} %bitcast.55), calls=%async_computation | async-start | bytes 8388608 | tf_op jit(solution)/shard_map/all_to_all | solution.py:23
  23.0 213.6 %all-gather.9.cloned.1.call-start = ((), (), s32[]{:S(2)}) async-start(), calls=%async_computation.2 | async-start | bytes 1392640 | tf_op jit(solution)/shard_map/all_gather | solution.py:24
  23.7 319.7 %all-gather.11.cloned.1.call-start = ((), (), s32[]{:S(2)}) async-start(), calls=%async_computation.3 | async-start | bytes 5406720 | tf_op jit(solution)/shard_map/all_gather | solution.py:55
  24.0 129.5 %copy-start.2 = (bf16[1,2,160,160]{3,2,1,0:T(8,128)(2,1)S(1)}, bf16[1,2,160,160]{3,2,1,0:T(8,128)(2,1)}, u32[]{:S(2)}) copy-start(bf16[1,2,160,160]{3,2,1,0:T(8,128)(2,1)} %param.11) | copy-start | bytes 307204
  24.0 211.5 %copy-start.1 = (bf16[1,160,512]{2,1,0:T(8,128)(2,1)S(1)}, bf16[1,160,512]{2,1,0:T(8,128)(2,1)}, u32[]{:S(2)}) copy-start(bf16[1,160,512]{2,1,0:T(8,128)(2,1)} %param.7) | copy-start | bytes 491524
  343.5 90.5 %copy-start.4 = (s32[1,32]{1,0:T(1,128)S(1)}, s32[1,32]{1,0:T(1,128)}, u32[]{:S(2)}) copy-start(s32[1,32]{1,0:T(1,128)} %param.13) | copy-start | bytes 388
Sparse Core Ops, SparseCore 0:
  10.1 138.8 all-gather.6
  151.0 73.8 all-gather.8
  236.7 106.7 all-gather.10
where the time goes:
time: 442 us; the launch traced here: 441 us
  waiting for transfers between devices  219 us (50%)
  blocking collectives  154 us (35%)
  matrix products  27.7 us (6%)
  local copies, waits for them, and re-layouts  17.2 us (4%)
  between operations  13.9 us (3%)
  starting transfers between devices  8.77 us (2%)
    all_gather x1, waiting for transfers between devices, on_device(): grad_rows = lax.all_gather(grad_in[0], 'tp', axis=1, tiled=True)  125 us
    all_gather x1, waiting for transfers between devices, on_device(): lax.all_gather(target_row[None], 'section', axis=0, tiled=True)  92.8 us
    psum x1, blocking collectives, on_device(): summed = lax.psum(slots, 'tp')  78.9 us
    psum x1, blocking collectives, on_device(): totals = lax.psum(partial_scores, 'tp')  75.6 us
    dot_general x1, matrix products, on_device(): lax.dot_general(delta.reshape(HEADS, tokens * local_width), target_rows.r...  15 us
  transfers between devices with their start and end apart: 4, of which 2 were waited for; matrix products, arithmetic and copies ran while one was open for 7% of the time, Pallas kernels for 0%

commit v1 on v0

--- a/solution.py
+++ b/solution.py
@@ -52,7 +52,10 @@
     )
     residual_grad = (grad_in[0].astype(jnp.float32) + increment).astype(jnp.bfloat16)
     target_row = increment.astype(jnp.bfloat16)
-    target_rows = lax.all_gather(target_row[None], "section", axis=0, tiled=True)
+    target_rows = jnp.concatenate(
+        lax.all_to_all(jnp.stack([target_row[None]] * lax.axis_size("section")), "section", 0, 0),
+        axis=0,
+    )
     delta = jnp.einsum(
         "thc,hcd->htd",
         all_delta_cols.reshape(tokens, HEADS, HEAD_DIM),

time: 442 us -> 597 us (1.35)
  the two profiles are of different devices: /device:TPU:8 before, /device:TPU:128 now
where the time goes in v1:
time: 597 us; the launch traced here: 596 us
  waiting for transfers between devices  346 us (58%)
  blocking collectives  175 us (29%)
  local copies, waits for them, and re-layouts  26.7 us (4%)
  starting transfers between devices  21.9 us (4%)
  between operations  14.2 us (2%)
  matrix products  11.8 us (2%)
    all_gather x1, waiting for transfers between devices, on_device(): all_delta_cols = lax.all_gather(head_delta[0], 'tp', axis=1, tiled=True)  219 us
    all_gather x1, waiting for transfers between devices, on_device(): grad_rows = lax.all_gather(grad_in[0], 'tp', axis=1, tiled=True)  126 us
    psum x1, blocking collectives, on_device(): totals = lax.psum(partial_scores, 'tp')  97.4 us
    psum x1, blocking collectives, on_device(): summed = lax.psum(slots, 'tp')  77.9 us
    unnamed x16, local copies, waits for them, and re-layouts  16.7 us
    all_to_all x1, starting transfers between devices, on_device(): lax.all_to_all(jnp.stack([target_row[None]] * lax.axis_size('section')),...  13 us
  transfers between devices with their start and end apart: 4, of which 2 were waited for; matrix products, arithmetic and copies ran while one was open for 3% of the time, Pallas kernels for 0%

profile of v1, /device:TPU:128, one launch (start us, length us, event | category | flops | bytes accessed | tf_op | source)
XLA Modules:
  0.0 596.4 jit_solution(16338059644333020521)
XLA Ops:
  7.2 0.0 copy-start
  7.2 4.1 copy.20
  11.3 4.3 copy.36
  15.6 8.6 %all-to-all-start = ((bf16[16,256,512]{2,1,0:T(8,128)(2,1)}), bf16[16,256,512]{2,1,0:T(8,128)(2,1)}, u32[]{:S(2)}, u32[]{:S(2)}) async-start(bf16[16,256,512]{2,1,0:T(8,128)(2,1)} %bitcast.65), calls=%async_computation | async-start | bytes 8388608 | tf_op jit(solution)/shard_map/all_to_all | solution.py:23
  24.3 0.0 all-gather.5.cloned.1.call-start
  24.3 0.7 all-gather.5.cloned.1.call-update
  25.1 0.1 and_convert_fusion
  25.2 0.0 copy-start.3
  25.2 0.0 copy-start.2
  25.2 125.8 %all-gather.5.cloned.1.call-done = bf16[1,160,8192]{2,1,0:T(8,128)(2,1)} async-done(((bf16[1,160,512]{2,1,0:T(8,128)(2,1)}), bf16[1,160,8192]{2,1,0:T(8,128)(2,1)}) %all-gather.5.cloned.1.call-update) | async-done | bytes 2621456 | tf_op jit(solution)/shard_map/all_gather | solution.py:33
  151.0 4.5 fusion.11
  155.5 0.0 copy-done.3
  155.6 0.2 fusion.10
  155.9 2.7 dynamic_update_slice.3
  158.6 77.9 %all-reduce.1 = bf16[160,4,128]{2,1,0:T(4,128)(2,1)S(1)} all-reduce(f32[160,4,128]{2,1,0:T(4,128)S(1)} %dynamic_update_slice.3), channel_id=1, replica_groups=mesh['section'=32,'tp'=16] {'tp'}, use_global_device_ids=true, to_apply=%region_1.2 | all-reduce | flops 81920 | bytes 491520 | tf_op jit(solution)/shard_map/psum | solution.py:48
  236.5 0.0 copy-done
  236.5 1.0 fusion.33
  237.5 0.0 all-to-all-done
  237.5 2.9 stack.3
  240.5 13.0 %all-to-all-start.1 = ((bf16[32,1,160,512]{3,2,1,0:T(8,128)(2,1)}), bf16[32,1,160,512]{3,2,1,0:T(8,128)(2,1)}, u32[]{:S(2)}, u32[]{:S(2)}) async-start(bf16[32,1,160,512]{3,2,1,0:T(8,128)(2,1)} %stack.3), calls=%async_computation.1 | async-start | bytes 10485760 | tf_op jit(solution)/shard_map/all_to_all | solution.py:56
  253.4 0.2 all-gather.7.cloned.1.call-start
  253.7 0.5 all-gather.7.cloned.1.call-update
  254.2 219.3 %all-gather.7.cloned.1.call-done = bf16[1,160,4096]{2,1,0:T(8,128)(2,1)} async-done(((bf16[1,160,256]{2,1,0:T(8,128)(2,1)}), bf16[1,160,4096]{2,1,0:T(8,128)(2,1)}) %all-gather.7.cloned.1.call-update) | async-done | bytes 1310736 | tf_op jit(solution)/shard_map/all_gather | solution.py:24
  473.5 1.6 copy.19
  475.1 3.7 convolution_convert_fusion
  478.8 5.3 copy.21
  484.2 0.0 all-to-all-done.1
  484.2 5.6 copy.22
  489.8 0.0 copy-start.5
  489.8 1.5 fusion.38
  491.3 97.4 %psum.15 = f32[32,32]{1,0:T(8,128)S(1)} all-reduce(f32[32,32]{1,0:T(8,128)S(1)} %fusion.38), channel_id=1, replica_groups=mesh['section'=32,'tp'=16] {'tp'}, use_global_device_ids=true, to_apply=%region_2.3 | all-reduce | flops 1024 | bytes 8192 | tf_op jit(solution)/shard_map/psum | solution.py:71
  588.7 0.9 convolution_bitcast_fusion
  (10 shorter events, 0.1 us)
Async XLA Ops:
  7.2 229.3 %copy-start = (bf16[1,512,512]{2,1,0:T(8,128)(2,1)S(1)}, bf16[1,512,512]{2,1,0:T(8,128)(2,1)}, u32[]{:S(2)}) copy-start(bf16[1,512,512]{2,1,0:T(8,128)(2,1)} %param.9) | copy-start | bytes 1572868
  15.6 9.4 %copy-start.4 = (s32[160]{0:T(256)S(1)}, s32[160]{0:T(256)}, u32[]{:S(2)}) copy-start(s32[160]{0:T(256)} %param.12) | copy-start | bytes 1924
  15.6 221.9 %all-to-all-start = ((bf16[16,256,512]{2,1,0:T(8,128)(2,1)}), bf16[16,256,512]{2,1,0:T(8,128)(2,1)}, u32[]{:S(2)}, u32[]{:S(2)}) async-start(bf16[16,256,512]{2,1,0:T(8,128)(2,1)} %bitcast.65), calls=%async_computation | async-start | bytes 8388608 | tf_op jit(solution)/shard_map/all_to_all | solution.py:23
  24.3 126.7 %all-gather.5.cloned.1.call-start = ((), (), s32[]{:S(2)}) async-start(), calls=%async_computation.2 | async-start | bytes 2785280 | tf_op jit(solution)/shard_map/all_gather | solution.py:33
  25.2 130.4 %copy-start.3 = (bf16[1,2,160,160]{3,2,1,0:T(8,128)(2,1)S(1)}, bf16[1,2,160,160]{3,2,1,0:T(8,128)(2,1)}, u32[]{:S(2)}) copy-start(bf16[1,2,160,160]{3,2,1,0:T(8,128)(2,1)} %param.11) | copy-start | bytes 307204
  25.2 211.3 %copy-start.2 = (bf16[1,160,512]{2,1,0:T(8,128)(2,1)S(1)}, bf16[1,160,512]{2,1,0:T(8,128)(2,1)}, u32[]{:S(2)}) copy-start(bf16[1,160,512]{2,1,0:T(8,128)(2,1)} %param.7) | copy-start | bytes 491524
  240.5 243.7 %all-to-all-start.1 = ((bf16[32,1,160,512]{3,2,1,0:T(8,128)(2,1)}), bf16[32,1,160,512]{3,2,1,0:T(8,128)(2,1)}, u32[]{:S(2)}, u32[]{:S(2)}) async-start(bf16[32,1,160,512]{3,2,1,0:T(8,128)(2,1)} %stack.3), calls=%async_computation.1 | async-start | bytes 10485760 | tf_op jit(solution)/shard_map/all_to_all | solution.py:56
  253.4 220.1 %all-gather.7.cloned.1.call-start = ((), (), s32[]{:S(2)}) async-start(), calls=%async_computation.3 | async-start | bytes 1392640 | tf_op jit(solution)/shard_map/all_gather | solution.py:24
  484.2 5.6 copy-start.1
  489.8 98.9 %copy-start.5 = (s32[1,32]{1,0:T(1,128)S(1)}, s32[1,32]{1,0:T(1,128)}, u32[]{:S(2)}) copy-start(s32[1,32]{1,0:T(1,128)} %param.13) | copy-start | bytes 388
Sparse Core Ops, SparseCore 0:
  27.2 123.7 all-gather.4
  256.3 217.1 all-gather.6
